TPU v7x, 256 devices: a whole 4x4x8 slice. The times are simulated.
256 devices in a mesh: dp: 16 (over y_lo, z), fsdp: 16 (over x, y_hi, core).
Axes of the slice: x: 4, y: 4 (y_hi: 2, y_lo: 2; y = y_hi * 2 + y_lo), z: 8, core: 2. Of those that a mesh axis runs over, the one named last changes fastest.
Arguments:
- latents: bfloat16 [1024, 8, 8, 640], P(('dp', 'fsdp'))
- bucket: int32 [1024], P(('dp', 'fsdp')), may hold values from 0 to 39
- cotangent: bfloat16 [1024, 4, 4, 640], P(('dp', 'fsdp')), may hold values from -6 to 6
- tile_count: int32 [256], P(('dp', 'fsdp')), may hold values from 1 to 4, as said below
- cond_table: float32 [40, 640], replicated, may hold values from -3 to 3
- norm_gain: float32 [640], replicated, may hold values from 0.1 to 1.9
- norm_shift: float32 [640], replicated, may hold values from -3 to 3
- conv_bias: float32 [640], replicated, may hold values from -3 to 3
- down_bias: float32 [640], replicated, may hold values from -3 to 3
- conv_weight: bfloat16 [5760, 640], P('fsdp'), may hold values from -0.078125 to 0.078125
- down_weight: bfloat16 [5760, 640], P('fsdp'), may hold values from -0.078125 to 0.078125
Outputs:
- block_output: bfloat16 [1024, 4, 4, 640], P(('dp', 'fsdp'))
- grad_input: bfloat16 [1024, 8, 8, 640], P(('dp', 'fsdp'))
- grad_conv: float32 [5760, 640], P('fsdp')
- grad_affine: float32 [3, 640], replicated
Inputs may be any that keep to these rules, and one draw needn't show every extreme that they name: Slots 0 to tile_count - 1 of a device are live; some device holds exactly 4 live tiles.
All inputs are finite; a program needn't handle non-finite values.
Results may differ from a plain program's by a relative error of at most 0.005.
Values may be sent and summed in bfloat16 or wider, within the bound.
No kernel may reach another device: no remote copies, remote signals or barrier semaphores. Data moves between devices by JAX's collectives and lax.ppermute only.
A program may use at most 128 MiB of HBM per device.

v0:
```python
import math
import jax
import jax.numpy as jnp
from jax import lax
from jax.sharding import PartitionSpec as P

GROUPS = 32
CONV_DIMS = ("NHWC", "HWIO", "NHWC")
BACK_DIMS = ("NHWC", "HWOI", "NHWC")


def group_mean(channel_sums, per_group):
    tiles, channels = channel_sums.shape
    width = channels // GROUPS
    grouped = channel_sums.reshape(tiles, GROUPS, width).sum(axis=-1) / per_group
    return jnp.repeat(grouped, width, axis=1)


def shifted(padded, tap, tile_side):
    row_off = tap // 3
    col_off = tap % 3
    return lax.dynamic_slice(
        padded, (0, row_off, col_off, 0), (padded.shape[0], tile_side, tile_side, padded.shape[3])
    )


def body(
    latents,
    bucket,
    cotangent,
    tile_count,
    cond_table,
    norm_gain,
    norm_shift,
    conv_bias,
    down_bias,
    conv_weight,
    down_weight,
):
    slot_total, tile_side, _, channels = latents.shape
    row_block = conv_weight.shape[0]
    conv_full = lax.all_gather(conv_weight, "fsdp", axis=0, tiled=True)
    down_full = lax.all_gather(down_weight, "fsdp", axis=0, tiled=True)
    conv_kernel = conv_full.reshape(3, 3, channels, channels)
    down_kernel = down_full.reshape(3, 3, channels, channels)
    live = jnp.arange(slot_total, dtype=jnp.int32) < tile_count[0]
    live4 = live[:, None, None, None]
    masked_cot = jnp.where(live4, cotangent, jnp.zeros_like(cotangent))
    per_group = tile_side * tile_side * (channels // GROUPS)
    values = latents.astype(jnp.float32)
    center = group_mean(jnp.sum(values, axis=(1, 2)), per_group)
    deviation = values - center[:, None, None, :]
    spread = group_mean(jnp.sum(deviation * deviation, axis=(1, 2)), per_group)
    inv_std = lax.rsqrt(spread + 1e-05)[:, None, None, :]
    normed = deviation * inv_std
    pre_act = normed * norm_gain + norm_shift
    sigmoid_v = jax.nn.sigmoid(pre_act)
    activated = (pre_act * sigmoid_v).astype(jnp.bfloat16)
    act_all = lax.all_gather(activated, "fsdp", axis=0, tiled=True)
    conditioning = cond_table[bucket]
    conv_out = lax.conv_general_dilated(
        activated,
        conv_kernel,
        (1, 1),
        ((1, 1), (1, 1)),
        dimension_numbers=CONV_DIMS,
        preferred_element_type=jnp.float32,
    )
    conv_out = conv_out + conv_bias + conditioning[:, None, None, :]
    residual = (values + conv_out).astype(jnp.bfloat16)
    down_out = lax.conv_general_dilated(
        residual,
        down_kernel,
        (2, 2),
        ((1, 1), (1, 1)),
        dimension_numbers=CONV_DIMS,
        preferred_element_type=jnp.float32,
    )
    block_output = (down_out + down_bias).astype(jnp.bfloat16)
    block_output = jnp.where(live4, block_output, jnp.zeros_like(block_output))
    grad_resid = lax.conv_general_dilated(
        masked_cot,
        down_kernel[::-1, ::-1],
        (1, 1),
        ((1, 2), (1, 2)),
        lhs_dilation=(2, 2),
        dimension_numbers=BACK_DIMS,
        preferred_element_type=jnp.float32,
    )
    grad_hidden = grad_resid.astype(jnp.bfloat16)
    grad_act = lax.conv_general_dilated(
        grad_hidden,
        conv_kernel[::-1, ::-1],
        (1, 1),
        ((1, 1), (1, 1)),
        dimension_numbers=BACK_DIMS,
        preferred_element_type=jnp.float32,
    )
    grad_pre = grad_act * sigmoid_v * (1.0 + pre_act * (1.0 - sigmoid_v))
    scaled = grad_pre * norm_gain
    mean_one = group_mean(jnp.sum(scaled, axis=(1, 2)), per_group)[:, None, None, :]
    mean_two = group_mean(jnp.sum(scaled * normed, axis=(1, 2)), per_group)[:, None, None, :]
    grad_input = (grad_resid + inv_std * (scaled - mean_one - normed * mean_two)).astype(
        jnp.bfloat16
    )
    affine = jnp.stack(
        [
            jnp.sum(grad_pre * normed, axis=(0, 1, 2)),
            jnp.sum(grad_pre, axis=(0, 1, 2)),
            jnp.sum(grad_resid, axis=(0, 1, 2)),
        ]
    )
    affine_hi = affine.astype(jnp.bfloat16)
    affine_lo = (affine - affine_hi.astype(jnp.float32)).astype(jnp.bfloat16)
    hid_rows = grad_hidden.reshape(-1, channels)
    sent = jnp.concatenate([hid_rows, affine_hi, affine_lo], axis=0)
    sent_all = lax.all_gather(sent, "fsdp", axis=0, tiled=False)
    hid_all = sent_all[:, : hid_rows.shape[0]].reshape(-1, channels)
    affine_parts = sent_all[:, hid_rows.shape[0] :].astype(jnp.float32)
    affine_fsdp = jnp.sum(affine_parts[:, :3] + affine_parts[:, 3:], axis=0)
    first_row = lax.axis_index("fsdp") * row_block
    first_tap = first_row // channels
    first_chan = first_row % channels
    span = (row_block + channels - 1) // channels + 1
    act_pad = jnp.pad(act_all, ((0, 0), (1, 1), (1, 1), (0, 0)))
    taps = [shifted(act_pad, jnp.minimum(first_tap + extra, 8), tile_side) for extra in range(span)]
    tap_cols = jnp.concatenate(taps, axis=-1)
    own_cols = lax.dynamic_slice_in_dim(tap_cols, first_chan, row_block, axis=3)
    weight_term = lax.dot_general(
        own_cols.reshape(-1, row_block),
        hid_all,
        (((0,), (0,)), ((), ())),
        preferred_element_type=jnp.float32,
    )
    loss_scale = 4.0 / math.sqrt(
        tile_side * tile_side * slot_total * lax.axis_size("dp") * lax.axis_size("fsdp")
    )
    summed = lax.psum(jnp.concatenate([weight_term, affine_fsdp], axis=0) * loss_scale, "dp")
    grad_conv = summed[:row_block]
    grad_affine = summed[row_block:]
    return (block_output, grad_input, grad_conv, grad_affine)


def solution(mesh):
    placed = (
        P(("dp", "fsdp"), None, None, None),
        P(("dp", "fsdp")),
        P(("dp", "fsdp"), None, None, None),
        P(("dp", "fsdp")),
        P(),
        P(),
        P(),
        P(),
        P(),
        P("fsdp", None),
        P("fsdp", None),
    )
    return jax.shard_map(
        body,
        mesh=mesh,
        in_specs=placed,
        out_specs=(
            P(("dp", "fsdp"), None, None, None),
            P(("dp", "fsdp"), None, None, None),
            P("fsdp", None),
            P(),
        ),
        check_vma=False,
    )
```

profile of v0, /device:TPU:2, one launch (start us, length us, event | category | flops | bytes accessed | tf_op | source)
XLA Modules:
  0.0 456.9 jit_solution(273286597701240359)
XLA Ops:
  7.3 0.7 all-gather.9.cloned.1.call-update
  8.0 0.7 all-gather.7.cloned.1.call-update
  9.4 1.2 convert_reduce_fusion
  10.9 0.1 sub.39
  11.0 1.3 fusion.20
  12.6 0.1 rsqrt.12
  12.8 73.6 %all-gather.9.cloned.1.call-done = bf16[5760,640]{1,0:T(8,128)(2,1)} async-done(((bf16[360,640]{1,0:T(8,128)(2,1)}), bf16[5760,640]{1,0:T(8,128)(2,1)}) %all-gather.9.cloned.1.call-update) | async-done | bytes 7372816 | tf_op jit(solution)/shard_map/all_gather | solution.py:43
  86.4 5.5 %fusion.28 = (bf16[4,8,8,640]{3,0,2,1:T(4,128)(2,1)S(1)}, f32[4,8,8,640]{3,0,2,1:T(4,128)S(1)}) fusion(bf16[3,3,640,640]{3,2,1,0:T(8,128)(2,1)} %bitcast.23, bf16[4,4,4,640]{3,2,1,0:T(4,128)(2,1)} %param.13, pred[4]{0:T(512)(128)(4,1)S(1)} %iota_compare_fusion), kind=kOutput, calls=%fused_computation.55 | convolution fusion | flops 396697600 | bytes 8437764 | tf_op jit(solution)/shard_map/conv_general_dilated | solution.py:81
  91.8 69.0 %all-gather.7.cloned.1.call-done = bf16[5760,640]{1,0:T(8,128)(2,1)} async-done(((bf16[360,640]{1,0:T(8,128)(2,1)}), bf16[5760,640]{1,0:T(8,128)(2,1)}) %all-gather.7.cloned.1.call-update) | async-done | bytes 7372816 | tf_op jit(solution)/shard_map/all_gather | solution.py:42
  160.8 7.6 %fusion.19 = (f32[640]{0:T(1024)S(1)}, f32[4,640]{1,0:T(4,128)S(1)}, f32[4,640]{1,0:T(4,128)S(1)}, f32[640]{0:T(1024)S(1)}, f32[4,8,8,640]{3,0,2,1:T(4,128)S(1)}) fusion(f32[4,640]{1,0:T(4,128)S(1)} %rsqrt.12, f32[4,640]{1,0:T(4,128)S(1)} %sub.39, bf16[4,8,8,640]{3,2,1,0:T(8,128)(2,1)S(1)} %copy-done.1, f32[640]{0:T(1024)S(1)} %copy-done.4, ...), kind=kOutput, calls=%fused_computation.30 | convolution fusion | flops 1589241600 | bytes 8734720 | tf_op jit(solution)/shard_map/conv_general_dilated | solution.py:91
  168.7 0.1 mul.79
  168.9 0.1 reshape.61
  169.2 0.1 sub.43
  169.3 1.6 fusion.27
  170.9 0.8 copy.27
  171.9 0.8 maximum_bitcast_fusion
  172.7 0.2 all-reduce.3.cloned.1.call-start
  173.1 0.6 gather_fusion
  173.7 62.0 %all-gather.11.cloned.1.call-done = bf16[64,8,8,640]{3,2,1,0:T(8,128)(2,1)} async-done(((bf16[4,8,8,640]{3,2,1,0:T(8,128)(2,1)}), bf16[64,8,8,640]{3,2,1,0:T(8,128)(2,1)}) %all-gather.11.cloned.1.call-update) | async-done | bytes 5242896 | tf_op jit(solution)/shard_map/all_gather | solution.py:59
  235.7 11.6 %pad_dynamic-slice_fusion = (bf16[64,8,8,640]{3,2,1,0:T(8,128)(2,1)}, bf16[64,8,8,640]{3,2,1,0:T(8,128)(2,1)}) fusion(s32[]{:T(128)S(6)} %select_n.59, s32[]{:T(128)S(6)} %select_n.61, bf16[64,8,8,640]{3,2,1,0:T(8,128)(2,1)} %all-gather.11.cloned.1.call-done, s32[]{:T(128)S(6)} %select_n.55, s32[]{:T(128)S(6)} %select_n.57), kind=kLoop, calls=%fused_computation.1 | loop fusion | bytes 15728656 | tf_op jit(solution)/shard_map/dynamic_slice | solution.py:22
  247.3 5.0 %fusion = bf16[64,8,8,360]{3,2,1,0:T(8,128)(2,1)S(1)} fusion(s32[]{:T(128)S(6)} %select_n.63, bf16[64,8,8,640]{3,2,1,0:T(8,128)(2,1)} %get-tuple-element.21, bf16[64,8,8,640]{3,2,1,0:T(8,128)(2,1)} %get-tuple-element.20), kind=kLoop, calls=%fused_computation.5 | loop fusion | flops 5898240 | bytes 13434884 | tf_op jit(solution)/shard_map/concatenate | solution.py:127
  252.3 51.1 %all-gather.13.cloned.1.call-done = bf16[16,262,640]{2,1,0:T(8,128)(2,1)} async-done(((bf16[1,262,640]{2,1,0:T(8,128)(2,1)}), bf16[16,262,640]{2,1,0:T(8,128)(2,1)}) %all-gather.13.cloned.1.call-update) | async-done | bytes 5365776 | tf_op jit(solution)/shard_map/all_gather | solution.py:117
  303.4 1.1 slice_convert_fusion
  304.5 1.4 slice-done
  305.9 2.5 fusion.29
  308.4 1.0 maximum_multiply_fusion
  309.5 12.0 %fusion.6 = bf16[4,4,4,640]{3,0,2,1:T(4,128)(2,1)S(1)} fusion(bf16[3,3,640,640]{3,2,1,0:T(8,128)(2,1)} %bitcast.24, f32[640]{0:T(1024)S(1)} %copy-done.5, pred[4]{0:T(512)(128)(4,1)S(1)} %iota_compare_fusion, bf16[3,3,640,640]{3,2,1,0:T(8,128)(2,1)} %bitcast.27, f32[4,640]{1,0:T(4,128)S(1)} %gather_fusion, f32[640]{0:T(1024)S(1)} %copy-done.6, ...), kind=kOutput, calls=%fused_computation.14 | convolution fusion | flops 1985044480 | bytes 15196164 | tf_op jit(solution)/shard_map/conv_general_dilated | solution.py:71
  321.6 0.7 copy.29
  322.2 0.8 copy.30
  323.0 123.9 %all-reduce.3.cloned.1.call-done = f32[363,640]{1,0:T(8,128)} async-done(((f32[363,640]{1,0:T(8,128)}), f32[363,640]{1,0:T(8,128)}) %all-reduce.3.cloned.1.call-update) | async-done | bytes 929296 | tf_op jit(solution)/shard_map/psum | solution.py:138
  446.8 1.3 slice.31
  448.2 2.2 slice.30
  (49 shorter events, 1.4 us)
Async XLA Ops:
  7.2 165.9 %copy-start = (f32[40,640]{1,0:T(8,128)S(1)}, f32[40,640]{1,0:T(8,128)}, u32[]{:S(2)}) copy-start(f32[40,640]{1,0:T(8,128)} %param.15) | copy-start | bytes 307204
  7.2 153.7 %copy-start.1 = (bf16[4,8,8,640]{3,2,1,0:T(8,128)(2,1)S(1)}, bf16[4,8,8,640]{3,2,1,0:T(8,128)(2,1)}, u32[]{:S(2)}) copy-start(bf16[4,8,8,640]{3,2,1,0:T(8,128)(2,1)} %param.11) | copy-start | bytes 983044
  7.2 153.6 %copy-start.3 = (f32[640]{0:T(1024)S(1)}, f32[640]{0:T(1024)}, u32[]{:S(2)}) copy-start(f32[640]{0:T(1024)} %param.17) | copy-start | bytes 7684
  7.2 153.6 %copy-start.4 = (f32[640]{0:T(1024)S(1)}, f32[640]{0:T(1024)}, u32[]{:S(2)}) copy-start(f32[640]{0:T(1024)} %param.16) | copy-start | bytes 7684
  7.2 79.1 %all-gather.9.cloned.1.call-start = ((), (), s32[]{:S(2)}) async-start(), calls=%async_computation.1 | async-start | bytes 7833600 | tf_op jit(solution)/shard_map/all_gather | solution.py:43
  7.9 152.9 %all-gather.7.cloned.1.call-start = ((), (), s32[]{:S(2)}) async-start(), calls=%async_computation | async-start | bytes 7833600 | tf_op jit(solution)/shard_map/all_gather | solution.py:42
  8.7 227.0 %all-gather.11.cloned.1.call-start = ((), (), s32[]{:S(2)}) async-start(), calls=%async_computation.2 | async-start | bytes 5570560 | tf_op jit(solution)/shard_map/all_gather | solution.py:59
  160.8 12.2 %copy-start.7 = (s32[4]{0:T(128)S(1)}, s32[4]{0:T(128)}, u32[]{:S(2)}) copy-start(s32[4]{0:T(128)} %param.12) | copy-start | bytes 52
  171.7 131.6 %all-gather.13.cloned.1.call-start = ((), (), s32[]{:S(2)}) async-start(), calls=%async_computation.4 | async-start | bytes 5744640 | tf_op jit(solution)/shard_map/all_gather | solution.py:117
  172.7 274.1 %all-reduce.3.cloned.1.call-start = ((), (), s32[]{:S(2)}) async-start(), calls=%async_computation.3 | async-start | bytes 1884160 | tf_op jit(solution)/shard_map/psum | solution.py:138
  303.3 2.6 slice-start
  305.9 3.6 copy-start.5
  305.9 3.6 copy-start.6
  309.5 12.7 %copy-start.2 = (bf16[4,8,8,640]{3,0,2,1:T(4,128)(2,1)S(1)}, bf16[4,8,8,640]{3,0,2,1:T(4,128)(2,1)}, u32[]{:S(2)}) copy-start(bf16[4,8,8,640]{3,0,2,1:T(4,128)(2,1)} %get-tuple-element.23) | copy-start | bytes 983044
Sparse Core Ops, SparseCore 0:
  10.8 75.4 all-gather.8
  89.2 71.6 all-gather.6
  171.9 63.7 all-gather.10
  238.9 64.4 all-gather.12
  309.6 137.2 all-reduce.2
where the time goes:
time: 457 us
  waiting for transfers between devices  381 us (83%)
  matrix products  27.6 us (6%)
  local copies, waits for them, and re-layouts  20.6 us (5%)
  between operations  14.8 us (3%)
  other arithmetic  12.5 us (3%)
    psum x1, waiting for transfers between devices, body(): lax.psum(jnp.concatenate([weight_term, affine_fsdp], axis=0) * loss_scale...  124 us
    all_gather x1, waiting for transfers between devices, body(): down_full = lax.all_gather(down_weight, 'fsdp', axis=0, tiled=True)  73.6 us
    all_gather x1, waiting for transfers between devices, body(): conv_full = lax.all_gather(conv_weight, 'fsdp', axis=0, tiled=True)  69 us
    all_gather x1, waiting for transfers between devices, body(): act_all = lax.all_gather(activated, 'fsdp', axis=0, tiled=True)  62 us
    all_gather x1, waiting for transfers between devices, body(): sent_all = lax.all_gather(sent, 'fsdp', axis=0, tiled=False)  51.1 us
    conv_general_dilated x1, matrix products, body(): lax.conv_general_dilated(residual, down_kernel, (2, 2), ((1, 1), (1, 1)),...  12 us
    dynamic_slice x1, local copies, waits for them, and re-layouts, shifted(): lax.dynamic_slice(padded, (0, row_off, col_off, 0), (padded.shape[0], til...  11.6 us
  transfers between devices with their start and end apart: 5, of which 5 were waited for; matrix products, arithmetic and copies ran while one was open for 9% of the time, Pallas kernels for 0%

commit v1 on v0

--- a/solution.py
+++ b/solution.py
@@ -135,7 +135,10 @@
     loss_scale = 4.0 / math.sqrt(
         tile_side * tile_side * slot_total * lax.axis_size("dp") * lax.axis_size("fsdp")
     )
-    summed = lax.psum(jnp.concatenate([weight_term, affine_fsdp], axis=0) * loss_scale, "dp")
+    summed = jnp.sum(
+        lax.all_gather(jnp.concatenate([weight_term, affine_fsdp], axis=0) * loss_scale, "dp"),
+        axis=0,
+    )
     grad_conv = summed[:row_block]
     grad_affine = summed[row_block:]
     return (block_output, grad_input, grad_conv, grad_affine)

time: 457 us -> 492 us (1.077)
  waiting for transfers between devices: 381 us -> 411 us
  other arithmetic: 12.5 us -> 18.6 us
    all_gather x0 -> x1, waiting for transfers between devices: none -> 153 us  [body(): lax.all_gather(jnp.concatenate([weight_term, affine_fsdp], axis=0) * loss...]
    psum x1 -> x0, waiting for transfers between devices: 124 us -> none  [body(): lax.psum(jnp.concatenate([weight_term, affine_fsdp], axis=0) * loss_scale...]
    reduce_sum x0 -> x1, other arithmetic: none -> 6.1 us  [body(): jnp.sum(lax.all_gather(jnp.concatenate([weight_term, affine_fsdp], axis=0...]
  transfers between devices with their start and end apart: 5 -> 5, of which waited for: 5 -> 5; matrix products, arithmetic and copies ran while one was open for 9% -> 8% of each run, Pallas kernels for 0% -> 0%
where the time goes in v1:
time: 492 us; the launch traced here: 491 us
  waiting for transfers between devices  411 us (84%)
  matrix products  27.6 us (6%)
  local copies, waits for them, and re-layouts  18.7 us (4%)
  other arithmetic  18.6 us (4%)
  between operations  14.8 us (3%)
    all_gather x1, waiting for transfers between devices, body(): lax.all_gather(jnp.concatenate([weight_term, affine_fsdp], axis=0) * loss...  153 us
    all_gather x1, waiting for transfers between devices, body(): down_full = lax.all_gather(down_weight, 'fsdp', axis=0, tiled=True)  73.6 us
    all_gather x1, waiting for transfers between devices, body(): conv_full = lax.all_gather(conv_weight, 'fsdp', axis=0, tiled=True)  69 us
    all_gather x1, waiting for transfers between devices, body(): act_all = lax.all_gather(activated, 'fsdp', axis=0, tiled=True)  62.6 us
    all_gather x1, waiting for transfers between devices, body(): sent_all = lax.all_gather(sent, 'fsdp', axis=0, tiled=False)  51.1 us
    conv_general_dilated x1, matrix products, body(): lax.conv_general_dilated(residual, down_kernel, (2, 2), ((1, 1), (1, 1)),...  12 us
    dynamic_slice x1, local copies, waits for them, and re-layouts, shifted(): lax.dynamic_slice(padded, (0, row_off, col_off, 0), (padded.shape[0], til...  11.6 us
  transfers between devices with their start and end apart: 5, of which 5 were waited for; matrix products, arithmetic and copies ran while one was open for 8% of the time, Pallas kernels for 0%

profile of v1, /device:TPU:2, one launch (start us, length us, event | category | flops | bytes accessed | tf_op | source)
XLA Modules:
  0.0 491.1 jit_solution(2496688177854236890)
XLA Ops:
  7.3 0.7 all-gather.10.cloned.1.call-update
  8.0 0.7 all-gather.8.cloned.1.call-update
  9.4 1.2 convert_reduce_fusion
  10.9 0.1 sub.39
  11.0 1.3 fusion.20
  12.6 0.1 rsqrt.12
  12.8 73.6 %all-gather.10.cloned.1.call-done = bf16[5760,640]{1,0:T(8,128)(2,1)} async-done(((bf16[360,640]{1,0:T(8,128)(2,1)}), bf16[5760,640]{1,0:T(8,128)(2,1)}) %all-gather.10.cloned.1.call-update) | async-done | bytes 7372816 | tf_op jit(solution)/shard_map/all_gather | solution.py:43
  86.4 5.5 %fusion.28 = (bf16[4,8,8,640]{3,0,2,1:T(4,128)(2,1)S(1)}, f32[4,8,8,640]{3,0,2,1:T(4,128)S(1)}) fusion(bf16[3,3,640,640]{3,2,1,0:T(8,128)(2,1)} %bitcast.26, bf16[4,4,4,640]{3,2,1,0:T(4,128)(2,1)} %param.13, pred[4]{0:T(512)(128)(4,1)S(1)} %iota_compare_fusion), kind=kOutput, calls=%fused_computation.56 | convolution fusion | flops 396697600 | bytes 8437764 | tf_op jit(solution)/shard_map/conv_general_dilated | solution.py:81
  91.8 69.0 %all-gather.8.cloned.1.call-done = bf16[5760,640]{1,0:T(8,128)(2,1)} async-done(((bf16[360,640]{1,0:T(8,128)(2,1)}), bf16[5760,640]{1,0:T(8,128)(2,1)}) %all-gather.8.cloned.1.call-update) | async-done | bytes 7372816 | tf_op jit(solution)/shard_map/all_gather | solution.py:42
  160.8 7.6 %fusion.19 = (f32[640]{0:T(1024)S(1)}, f32[4,640]{1,0:T(4,128)S(1)}, f32[4,640]{1,0:T(4,128)S(1)}, f32[640]{0:T(1024)S(1)}, f32[4,8,8,640]{3,0,2,1:T(4,128)S(1)}) fusion(f32[4,640]{1,0:T(4,128)S(1)} %rsqrt.12, f32[4,640]{1,0:T(4,128)S(1)} %sub.39, bf16[4,8,8,640]{3,2,1,0:T(8,128)(2,1)S(1)} %copy-done.1, f32[640]{0:T(1024)S(1)} %copy-done.4, ...), kind=kOutput, calls=%fused_computation.31 | convolution fusion | flops 1589241600 | bytes 8734720 | tf_op jit(solution)/shard_map/conv_general_dilated | solution.py:91
  168.7 0.1 mul.86
  169.2 0.1 sub.43
  169.3 1.6 fusion.27
  170.9 0.8 copy.27
  171.9 0.8 maximum_bitcast_fusion
  172.7 0.2 all-gather.14.cloned.1.call-start
  173.0 62.6 %all-gather.12.cloned.1.call-done = bf16[64,8,8,640]{3,2,1,0:T(8,128)(2,1)} async-done(((bf16[4,8,8,640]{3,2,1,0:T(8,128)(2,1)}), bf16[64,8,8,640]{3,2,1,0:T(8,128)(2,1)}) %all-gather.12.cloned.1.call-update) | async-done | bytes 5242896 | tf_op jit(solution)/shard_map/all_gather | solution.py:59
  235.6 11.6 %pad_dynamic-slice_fusion = (bf16[64,8,8,640]{3,2,1,0:T(8,128)(2,1)}, bf16[64,8,8,640]{3,2,1,0:T(8,128)(2,1)}) fusion(s32[]{:T(128)S(6)} %select_n.59, s32[]{:T(128)S(6)} %select_n.61, bf16[64,8,8,640]{3,2,1,0:T(8,128)(2,1)} %all-gather.12.cloned.1.call-done, s32[]{:T(128)S(6)} %select_n.55, s32[]{:T(128)S(6)} %select_n.57), kind=kLoop, calls=%fused_computation.1 | loop fusion | bytes 15728656 | tf_op jit(solution)/shard_map/dynamic_slice | solution.py:22
  247.3 5.0 %fusion = bf16[64,8,8,360]{3,2,1,0:T(8,128)(2,1)S(1)} fusion(s32[]{:T(128)S(6)} %select_n.63, bf16[64,8,8,640]{3,2,1,0:T(8,128)(2,1)} %get-tuple-element.21, bf16[64,8,8,640]{3,2,1,0:T(8,128)(2,1)} %get-tuple-element.20), kind=kLoop, calls=%fused_computation.5 | loop fusion | flops 5898240 | bytes 13434884 | tf_op jit(solution)/shard_map/concatenate | solution.py:127
  252.3 51.1 %all-gather.16.cloned.1.call-done = bf16[16,262,640]{2,1,0:T(8,128)(2,1)} async-done(((bf16[1,262,640]{2,1,0:T(8,128)(2,1)}), bf16[16,262,640]{2,1,0:T(8,128)(2,1)}) %all-gather.16.cloned.1.call-update) | async-done | bytes 5365776 | tf_op jit(solution)/shard_map/all_gather | solution.py:117
  303.3 1.1 slice_convert_fusion
  304.5 1.4 slice-done
  305.9 2.5 convolution_bitcast_fusion
  308.4 1.1 maximum_multiply_fusion
  309.6 0.6 gather_fusion
  310.2 12.0 %fusion.6 = bf16[4,4,4,640]{3,0,2,1:T(4,128)(2,1)S(1)} fusion(bf16[3,3,640,640]{3,2,1,0:T(8,128)(2,1)} %bitcast.27, f32[640]{0:T(1024)S(1)} %copy-done.5, pred[4]{0:T(512)(128)(4,1)S(1)} %iota_compare_fusion, bf16[3,3,640,640]{3,2,1,0:T(8,128)(2,1)} %bitcast.31, f32[4,640]{1,0:T(4,128)S(1)} %gather_fusion, f32[640]{0:T(1024)S(1)} %copy-done.6, ...), kind=kOutput, calls=%fused_computation.15 | convolution fusion | flops 1985044480 | bytes 15196164 | tf_op jit(solution)/shard_map/conv_general_dilated | solution.py:71
  322.2 0.7 copy.29
  322.9 0.8 copy.30
  323.6 153.2 %all-gather.14.cloned.1.call-done = f32[16,363,640]{2,1,0:T(8,128)} async-done(((f32[1,363,640]{2,1,0:T(8,128)}), f32[16,363,640]{2,1,0:T(8,128)}) %all-gather.14.cloned.1.call-update) | async-done | bytes 14868496 | tf_op jit(solution)/shard_map/all_gather | solution.py:139
  476.9 6.1 %reduce_sum.129 = f32[363,640]{1,0:T(8,128)S(1)} reduce(f32[16,363,640]{2,1,0:T(8,128)} %all-gather.14.cloned.1.call-done, f32[]{:T(128)} %constant.51.clone.1), dimensions={0}, to_apply=%region_12.13 | reduce | flops 3484800 | bytes 15797764 | tf_op jit(solution)/shard_map/reduce_sum | solution.py:138
  483.0 0.6 slice.31
  483.6 1.0 slice.30
  (50 shorter events, 1.5 us)
Async XLA Ops:
  7.2 302.4 %copy-start = (f32[40,640]{1,0:T(8,128)S(1)}, f32[40,640]{1,0:T(8,128)}, u32[]{:S(2)}) copy-start(f32[40,640]{1,0:T(8,128)} %param.15) | copy-start | bytes 307204
  7.2 153.7 %copy-start.1 = (bf16[4,8,8,640]{3,2,1,0:T(8,128)(2,1)S(1)}, bf16[4,8,8,640]{3,2,1,0:T(8,128)(2,1)}, u32[]{:S(2)}) copy-start(bf16[4,8,8,640]{3,2,1,0:T(8,128)(2,1)} %param.11) | copy-start | bytes 983044
  7.2 153.6 %copy-start.3 = (f32[640]{0:T(1024)S(1)}, f32[640]{0:T(1024)}, u32[]{:S(2)}) copy-start(f32[640]{0:T(1024)} %param.17) | copy-start | bytes 7684
  7.2 153.6 %copy-start.4 = (f32[640]{0:T(1024)S(1)}, f32[640]{0:T(1024)}, u32[]{:S(2)}) copy-start(f32[640]{0:T(1024)} %param.16) | copy-start | bytes 7684
  7.2 79.1 %all-gather.10.cloned.1.call-start = ((), (), s32[]{:S(2)}) async-start(), calls=%async_computation.1 | async-start | bytes 7833600 | tf_op jit(solution)/shard_map/all_gather | solution.py:43
  7.9 152.9 %all-gather.8.cloned.1.call-start = ((), (), s32[]{:S(2)}) async-start(), calls=%async_computation | async-start | bytes 7833600 | tf_op jit(solution)/shard_map/all_gather | solution.py:42
  8.7 227.0 %all-gather.12.cloned.1.call-start = ((), (), s32[]{:S(2)}) async-start(), calls=%async_computation.2 | async-start | bytes 5570560 | tf_op jit(solution)/shard_map/all_gather | solution.py:59
  171.7 131.6 %all-gather.16.cloned.1.call-start = ((), (), s32[]{:S(2)}) async-start(), calls=%async_computation.4 | async-start | bytes 5744640 | tf_op jit(solution)/shard_map/all_gather | solution.py:117
  172.7 304.2 %all-gather.14.cloned.1.call-start = ((), (), s32[]{:S(2)}) async-start(), calls=%async_computation.3 | async-start | bytes 16015360 | tf_op jit(solution)/shard_map/all_gather | solution.py:139
  303.3 2.6 slice-start
  305.9 3.6 copy-start.7
  305.9 4.2 copy-start.5
  305.9 4.2 copy-start.6
  310.2 12.7 %copy-start.2 = (bf16[4,8,8,640]{3,0,2,1:T(4,128)(2,1)S(1)}, bf16[4,8,8,640]{3,0,2,1:T(4,128)(2,1)}, u32[]{:S(2)}) copy-start(bf16[4,8,8,640]{3,0,2,1:T(4,128)(2,1)} %get-tuple-element.23) | copy-start | bytes 983044
Sparse Core Ops, SparseCore 0:
  10.8 75.4 all-gather.9
  89.2 71.6 all-gather.7
  171.8 63.7 all-gather.11
  238.9 64.4 all-gather.15
  309.6 167.1 all-gather.13
